TPU v7x, 32 devices: a whole 2x2x4 slice. The times are simulated.
32 devices in a mesh: seq: 4 (over z), ch: 8 (over y, x, core).
Axes of the slice: x: 2, y: 2, z: 4, core: 2. Of those that a mesh axis runs over, the one named last changes fastest.
Arguments:
- inputs: bfloat16 [1024, 8192], P('seq', 'ch'), may hold values from -6 to 6
- w_in: bfloat16 [3, 8192, 8192], P(None, 'seq', 'ch'), may hold values from -0.0625 to 0.0625
- short_filter: float32 [3, 3, 8192], P(None, None, 'ch'), may hold values from -3 to 3
- rates: float32 [16, 8192], P(None, 'ch'), may hold values from 9.765625e-05 to 0.05
- residues: float32 [16, 8192], P(None, 'ch'), may hold values from -3 to 3
- skip: float32 [8192], P('ch'), may hold values from -3 to 3
Outputs:
- gated: bfloat16 [1024, 8192], P('seq', 'ch')
All inputs are finite; a program needn't handle non-finite values.
Results may differ from a plain program's by a relative error of at most 0.0065.
Values may be sent and summed in bfloat16 or wider, within the bound.
No kernel may reach another device: no remote copies, remote signals or barrier semaphores. Data moves between devices by JAX's collectives and lax.ppermute only.
A program may use at most 128 MiB of HBM per device.

v0:
```python
import jax
import jax.numpy as jnp
from jax import lax
from jax.sharding import PartitionSpec as P

TAPS = 3


def passed_along(block, axis, distance):
    devices = range(lax.axis_size(axis))
    route = [(i - distance, i) for i in devices if i - distance in devices]
    return lax.ppermute(block, axis, route)


def carried_in(part, axis, combine, identity):
    place = lax.axis_index(axis)
    gathered = jax.tree.map(lambda a: lax.all_gather(a, axis), part)
    state = jax.tree.map(lambda a, e: jnp.zeros_like(a) + jnp.asarray(e, a.dtype), part, identity)

    def one(hop, state):
        return combine(
            state, jax.tree.map(lambda a: lax.dynamic_index_in_dim(a, hop, 0, False), gathered)
        )

    return lax.fori_loop(0, place, one, state)


def combine(earlier, later):
    return (earlier[0] * later[0], earlier[1] * later[0] + later[1])


def per_device(inputs, w_in, short_filter, rates, residues, skip):
    tok_rows = inputs.shape[0]
    width = w_in.shape[2]
    modes = rates.shape[0]
    features = lax.all_gather(inputs, "ch", axis=1, tiled=True)
    proj = jnp.einsum(
        "td,kdc->ktc",
        features,
        lax.all_gather(w_in, "seq", axis=1, tiled=True),
        preferred_element_type=jnp.float32,
    ).astype(jnp.bfloat16)
    prior = passed_along(proj[:, tok_rows - (TAPS - 1) :, :], "seq", 1)
    padded = jnp.concatenate([prior, proj], axis=1).astype(jnp.float32)
    mixed = jnp.zeros((3, tok_rows, width), jnp.float32)
    for j in range(TAPS):
        mixed = (
            mixed
            + short_filter[:, j, None, :] * padded[:, TAPS - 1 - j : TAPS - 1 - j + tok_rows, :]
        )
    query, key, value = (mixed[0], mixed[1], mixed[2])
    drive = key * value
    position = jnp.arange(tok_rows, dtype=jnp.float32)
    scaled = residues * jnp.sqrt(1.0 - jnp.exp(-2.0 * rates))
    end_powers = jnp.exp(-rates[None, :, :] * (tok_rows - 1.0 - position)[:, None, None])
    end_state = jnp.sum(end_powers * drive[:, None, :], axis=0)
    block_decay = jnp.exp(-rates * tok_rows)
    identity = (jnp.ones_like(block_decay), jnp.zeros_like(end_state))
    entering = carried_in((block_decay, end_state), "seq", combine, identity)[1]
    start_powers = jnp.exp(-rates[None, :, :] * (position + 1.0)[:, None, None])
    cross = jnp.sum(start_powers * (scaled * entering)[None, :, :], axis=1)
    center = (tok_rows - 1.0) / 2.0
    offset = (position - center)[:, None, None]
    rising = jnp.exp(rates[None, :, :] * offset) * drive[:, None, :]
    offsets = jnp.arange(tok_rows, dtype=jnp.int32)
    lower = (offsets[:, None] >= offsets[None, :]).astype(jnp.float32)
    prefix = jnp.dot(
        lower, rising.reshape(tok_rows, modes * width), precision=lax.Precision.HIGHEST
    )
    prefix = prefix.reshape(tok_rows, modes, width)
    falling = jnp.exp(-rates[None, :, :] * offset) * scaled[None, :, :]
    local = jnp.sum(falling * prefix, axis=1)
    return (query * (local + cross + skip[None, :] * drive)).astype(jnp.bfloat16)


def solution(mesh):
    in_specs = (
        P("seq", "ch"),
        P(None, "seq", "ch"),
        P(None, None, "ch"),
        P(None, "ch"),
        P(None, "ch"),
        P("ch"),
    )
    out_specs = P("seq", "ch")
    return jax.shard_map(
        per_device, mesh=mesh, in_specs=in_specs, out_specs=out_specs, check_vma=False
    )
```

profile of v0, /device:TPU:0, one launch (start us, length us, event | category | flops | bytes accessed | tf_op | source)
XLA Modules:
  0.0 979.4 jit_solution(17450163939474768816)
XLA Ops:
  6.5 0.7 all-gather.7.cloned.1.call-update
  7.3 0.0 all-gather.5.cloned.1.call-start
  7.3 0.7 all-gather.5.cloned.1.call-update
  8.0 0.9 fusion.17
  9.0 1.5 fusion.16
  10.5 38.1 %all-gather.7.cloned.1.call-done = bf16[256,8192]{1,0:T(8,128)(2,1)} async-done(((bf16[256,1024]{1,0:T(8,128)(2,1)}), bf16[256,8192]{1,0:T(8,128)(2,1)}) %all-gather.7.cloned.1.call-update) | async-done | bytes 4194320 | tf_op jit(solution)/shard_map/all_gather | solution.py:36
  48.6 837.6 %all-gather.5.cloned.1.call-done = bf16[3,8192,1024]{2,1,0:T(8,128)(2,1)} async-done(((bf16[3,2048,1024]{2,1,0:T(8,128)(2,1)}), bf16[3,8192,1024]{2,1,0:T(8,128)(2,1)}) %all-gather.5.cloned.1.call-update) | async-done | bytes 50331664 | tf_op jit(solution)/shard_map/all_gather | solution.py:40
  886.2 21.8 %fusion.7 = bf16[3,256,1024]{2,1,0:T(8,128)(2,1)S(1)} fusion(bf16[3,8192,1024]{2,1,0:T(8,128)(2,1)} %all-gather.5.cloned.1.call-done, bf16[256,8192]{1,0:T(8,128)(2,1)} %all-gather.7.cloned.1.call-done), kind=kOutput, calls=%fused_computation.15 | convolution fusion | flops 12885688320 | bytes 56098816 | tf_op jit(solution)/shard_map/td,kdc->ktc/dot_general | solution.py:37
  908.0 1.3 collective-permute-start
  909.3 14.3 %all-gather = f32[64,1024]{1,0:T(8,128)S(1)} all-gather(f32[16,1024]{1,0:T(8,128)S(1)} %get-tuple-element.63), channel_id=2, replica_groups=mesh['seq'=4,'ch'=8] {'seq'}, dimensions={0}, use_global_device_ids=true | all-gather | bytes 327680 | tf_op jit(solution)/shard_map/all_gather | solution.py:17
  923.6 0.6 copy.13
  924.3 0.5 maximum_convert_fusion
  924.7 0.9 fusion.2
  925.7 1.2 fusion.10
  926.8 2.5 copy.12
  929.4 4.1 multiply_reduce_fusion.1
  933.5 14.6 %all-gather.1 = f32[64,1024]{1,0:T(8,128)} all-gather(f32[16,1024]{1,0:T(8,128)S(1)} %multiply_reduce_fusion.1), channel_id=3, replica_groups=mesh['seq'=4,'ch'=8] {'seq'}, dimensions={0}, use_global_device_ids=true | all-gather | bytes 327680 | tf_op jit(solution)/shard_map/all_gather | solution.py:17
  948.1 0.2 while.12
  948.3 0.9 fusion.15
  949.2 3.9 bitcast_multiply_fusion.1
  953.1 0.0 copy-start.2
  953.1 14.0 %multiply_reduce_fusion.2 = f32[256,1024]{1,0:T(8,128)} fusion(f32[16,1024,256]{2,1,0:T(8,128)S(1)} %bitcast.50, f32[16,1024]{1,0:T(8,128)S(1)} %get-tuple-element.61, f32[256]{0:T(256)S(1)} %iota_add_fusion.1, f32[16,1024]{1,0:T(8,128)S(1)} %copy-done.1), kind=kOutput, calls=%fused_computation.5 | convolution fusion | flops 12901482496 | bytes 17957888 | tf_op jit(solution)/shard_map/dot_general | solution.py:67
  967.2 2.8 multiply_reduce_fusion
  970.0 2.6 fusion.12
  (14 shorter events, 0.1 us)
Async XLA Ops:
  6.5 42.0 %all-gather.7.cloned.1.call-start = ((), (), s32[]{:S(2)}) async-start(), calls=%async_computation.1 | async-start | bytes 4718592 | tf_op jit(solution)/shard_map/all_gather | solution.py:36
  7.3 878.9 %all-gather.5.cloned.1.call-start = ((), (), s32[]{:S(2)}) async-start(), calls=%async_computation | async-start | bytes 62914560 | tf_op jit(solution)/shard_map/all_gather | solution.py:40
  10.5 913.1 %copy-start = (f32[16,1024]{1,0:T(8,128)S(1)}, f32[16,1024]{1,0:T(8,128)}, u32[]{:S(2)}) copy-start(f32[16,1024]{1,0:T(8,128)} %param.11) | copy-start | bytes 196612
  908.0 16.3 %collective-permute-start = (bf16[3,2,1024]{2,1,0:T(2,128)(2,1)S(1)}, bf16[3,2,1024]{2,1,0:T(2,128)(2,1)S(1)}, u32[]{:S(2)}, u32[]{:S(2)}) collective-permute-start(bf16[3,2,1024]{2,1,0:T(2,128)(2,1)S(1)} %slice.40), channel_id=1, source_target_pairs={{0,8},{8,16},{16,24},{1,9},{9,17},{17,25},{2,10},{10,18},{18,26},{... | collective-permute-start | bytes 36872 | tf_op jit(solution)/shard_map/ppermute | solution.py:12
  948.3 4.8 copy-start.1
  953.1 16.9 %copy-start.2 = (f32[1024]{0:T(1024)S(1)}, f32[1024]{0:T(1024)}, u32[]{:S(2)}) copy-start(f32[1024]{0:T(1024)} %param.13) | copy-start | bytes 12292
Sparse Core Ops, SparseCore 0:
  9.2 39.2 all-gather.6
  50.1 835.9 all-gather.4
where the time goes:
time: 980 us; the launch traced here: 979 us
  waiting for transfers between devices  877 us (89%)
  matrix products  35.8 us (4%)
  blocking collectives  28.9 us (3%)
  other arithmetic  18.4 us (2%)
  between operations  13.5 us (1%)
    all_gather x1, waiting for transfers between devices, per_device(): lax.all_gather(w_in, 'seq', axis=1, tiled=True)  838 us
    all_gather x1, waiting for transfers between devices, per_device(): features = lax.all_gather(inputs, 'ch', axis=1, tiled=True)  38.1 us
    all_gather x2, blocking collectives, carried_in(): gathered = jax.tree.map(lambda a: lax.all_gather(a, axis), part)  28.9 us
    dot_general x1, matrix products, per_device(): jnp.einsum('td,kdc->ktc', features, lax.all_gather(w_in, 'seq', axis=1, t...  21.8 us
  transfers between devices with their start and end apart: 3, of which 2 were waited for; matrix products, arithmetic and copies ran while one was open for 0% of the time, Pallas kernels for 0%

commit v1 on v0

--- a/solution.py
+++ b/solution.py
@@ -4,6 +4,22 @@
 from jax.sharding import PartitionSpec as P
 
 TAPS = 3
+
+
+def ring_product(shard, axis, dim, term):
+    size, index, span = (lax.axis_size(axis), lax.axis_index(axis), shard.shape[dim])
+    right = [(i, (i + 1) % size) for i in range(size)]
+    behind = [(i, (i - 1) % size) for i in range(size)]
+    halfway = size // 2
+    from_left = from_right = shard
+    total = term(shard, index * span)
+    for lap in range(1, halfway + 1):
+        from_left = lax.ppermute(from_left, axis, right)
+        if lap < size - halfway:
+            from_right = lax.ppermute(from_right, axis, behind)
+            total = total + term(from_right, (index + lap) % size * span)
+        total = total + term(from_left, (index - lap) % size * span)
+    return total
 
 
 def passed_along(block, axis, distance):
@@ -34,11 +50,16 @@
     width = w_in.shape[2]
     modes = rates.shape[0]
     features = lax.all_gather(inputs, "ch", axis=1, tiled=True)
-    proj = jnp.einsum(
-        "td,kdc->ktc",
-        features,
-        lax.all_gather(w_in, "seq", axis=1, tiled=True),
-        preferred_element_type=jnp.float32,
+    proj = ring_product(
+        w_in,
+        "seq",
+        1,
+        lambda shard, at: jnp.einsum(
+            "td,kdc->ktc",
+            lax.dynamic_slice_in_dim(features, at, shard.shape[1], axis=1),
+            shard,
+            preferred_element_type=jnp.float32,
+        ),
     ).astype(jnp.bfloat16)
     prior = passed_along(proj[:, tok_rows - (TAPS - 1) :, :], "seq", 1)
     padded = jnp.concatenate([prior, proj], axis=1).astype(jnp.float32)

time: 980 us -> 901 us (0.919)
  waiting for transfers between devices: 877 us -> 788 us
    all_gather x1 -> x0, waiting for transfers between devices: 838 us -> none  [per_device(): lax.all_gather(w_in, 'seq', axis=1, tiled=True)]
    ppermute x0 -> x3, waiting for transfers between devices: none -> 485 us  [the longest x2 485 us: ring_product(): from_left = lax.ppermute(from_left, axis, right)]
    all_gather x1, waiting for transfers between devices: 38.1 us -> 302 us  [per_device(): features = lax.all_gather(inputs, 'ch', axis=1, tiled=True)]
    dot_general x1 -> x4, matrix products: 21.8 us -> 28.1 us  [per_device(): jnp.einsum('td,kdc->ktc', lax.dynamic_slice_in_dim(features, at, shard.sh...]
  transfers between devices with their start and end apart: 3 -> 5, of which waited for: 2 -> 3; matrix products, arithmetic and copies ran while one was open for 0% -> 3% of each run, Pallas kernels for 0% -> 0%
where the time goes in v1:
time: 901 us; the launch traced here: 900 us
  waiting for transfers between devices  788 us (87%)
  matrix products  42 us (5%)
  blocking collectives  28.5 us (3%)
  other arithmetic  17.1 us (2%)
  between operations  13.6 us (2%)
    ppermute x2, waiting for transfers between devices, ring_product(): from_left = lax.ppermute(from_left, axis, right)  485 us
    all_gather x1, waiting for transfers between devices, per_device(): features = lax.all_gather(inputs, 'ch', axis=1, tiled=True)  302 us
    all_gather x2, blocking collectives, carried_in(): gathered = jax.tree.map(lambda a: lax.all_gather(a, axis), part)  28.5 us
    dot_general x4, matrix products, per_device(): jnp.einsum('td,kdc->ktc', lax.dynamic_slice_in_dim(features, at, shard.sh...  28.1 us
  transfers between devices with their start and end apart: 5, of which 3 were waited for; matrix products, arithmetic and copies ran while one was open for 3% of the time, Pallas kernels for 0%

profile of v1, /device:TPU:0, one launch (start us, length us, event | category | flops | bytes accessed | tf_op | source)
XLA Modules:
  0.0 900.0 jit_solution(4827386025260264607)
XLA Ops:
  6.5 3.1 collective-permute-start.1
  9.6 2.0 collective-permute-start
  11.6 271.5 %collective-permute-done.1 = bf16[3,2048,1024]{2,1,0:T(8,128)(2,1)} collective-permute-done((bf16[3,2048,1024]{2,1,0:T(8,128)(2,1)}, bf16[3,2048,1024]{2,1,0:T(8,128)(2,1)}, u32[]{:S(2)}, u32[]{:S(2)}) %collective-permute-start.1) | collective-permute-done | bytes 12582944 | tf_op jit(solution)/shard_map/ppermute | solution.py:17
  283.3 0.9 fusion.25
  284.3 1.5 fusion.24
  285.7 302.2 %all-gather.4.cloned.1.call-done = bf16[256,8192]{1,0:T(8,128)(2,1)} async-done(((bf16[256,1024]{1,0:T(8,128)(2,1)}), bf16[256,8192]{1,0:T(8,128)(2,1)}) %all-gather.4.cloned.1.call-update) | async-done | bytes 4194320 | tf_op jit(solution)/shard_map/all_gather | solution.py:52
  587.9 6.9 fusion.11
  594.8 6.4 fusion.7
  601.3 6.4 fusion.9
  607.7 213.9 %collective-permute-done.2 = bf16[3,2048,1024]{2,1,0:T(8,128)(2,1)} collective-permute-done((bf16[3,2048,1024]{2,1,0:T(8,128)(2,1)}, bf16[3,2048,1024]{2,1,0:T(8,128)(2,1)}, u32[]{:S(2)}, u32[]{:S(2)}) %collective-permute-start.2) | collective-permute-done | bytes 12582944 | tf_op jit(solution)/shard_map/ppermute | solution.py:17
  821.6 8.3 fusion.2
  830.0 1.6 collective-permute-start.3
  831.6 14.0 %all-gather = f32[64,1024]{1,0:T(8,128)S(1)} all-gather(f32[16,1024]{1,0:T(8,128)S(1)} %get-tuple-element.63), channel_id=2, replica_groups=mesh['seq'=4,'ch'=8] {'seq'}, dimensions={0}, use_global_device_ids=true | all-gather | bytes 327680 | tf_op jit(solution)/shard_map/all_gather | solution.py:33
  845.6 0.6 copy.13
  846.7 0.9 fusion
  847.6 1.2 fusion.3
  848.8 2.5 copy.12
  851.3 4.1 multiply_reduce_fusion.1
  855.4 14.5 %all-gather.1 = f32[64,1024]{1,0:T(8,128)} all-gather(f32[16,1024]{1,0:T(8,128)S(1)} %multiply_reduce_fusion.1), channel_id=3, replica_groups=mesh['seq'=4,'ch'=8] {'seq'}, dimensions={0}, use_global_device_ids=true | all-gather | bytes 327680 | tf_op jit(solution)/shard_map/all_gather | solution.py:33
  870.2 0.9 fusion.23
  871.1 3.9 bitcast_multiply_fusion.1
  875.0 14.0 %multiply_reduce_fusion.2 = f32[256,1024]{1,0:T(8,128)} fusion(f32[16,1024,256]{2,1,0:T(8,128)S(1)} %bitcast.58, f32[16,1024]{1,0:T(8,128)S(1)} %get-tuple-element.61, f32[256]{0:T(256)S(1)} %iota_add_fusion.1, f32[16,1024]{1,0:T(8,128)S(1)} %copy-done.4), kind=kOutput, calls=%fused_computation.5 | convolution fusion | flops 12901482496 | bytes 17957888 | tf_op jit(solution)/shard_map/dot_general | solution.py:88
  889.0 2.8 multiply_reduce_fusion
  891.8 1.4 fusion.5
  (26 shorter events, 0.8 us)
Async XLA Ops:
  6.5 581.4 %all-gather.4.cloned.1.call-start = ((), (), s32[]{:S(2)}) async-start(), calls=%async_computation | async-start | bytes 4718592 | tf_op jit(solution)/shard_map/all_gather | solution.py:52
  6.5 276.6 %collective-permute-start.1 = (bf16[3,2048,1024]{2,1,0:T(8,128)(2,1)}, bf16[3,2048,1024]{2,1,0:T(8,128)(2,1)}, u32[]{:S(2)}, u32[]{:S(2)}) collective-permute-start(bf16[3,2048,1024]{2,1,0:T(8,128)(2,1)} %param.9), channel_id=1, source_target_pairs={{0,8},{8,16},{16,24},{24,0},{1,9},{9,17},{17,25},{25,1},{2,10},{10... | collective-permute-start | bytes 37748744 | tf_op jit(solution)/shard_map/ppermute | solution.py:17
  9.6 591.7 %collective-permute-start = (bf16[3,2048,1024]{2,1,0:T(8,128)(2,1)}, bf16[3,2048,1024]{2,1,0:T(8,128)(2,1)}, u32[]{:S(2)}, u32[]{:S(2)}) collective-permute-start(bf16[3,2048,1024]{2,1,0:T(8,128)(2,1)} %param.9), channel_id=1, source_target_pairs={{0,24},{8,0},{16,8},{24,16},{1,25},{9,1},{17,9},{25,17},{2,26},{10... | collective-permute-start | bytes 37748744 | tf_op jit(solution)/shard_map/ppermute | solution.py:19
  283.2 538.4 %collective-permute-start.2 = (bf16[3,2048,1024]{2,1,0:T(8,128)(2,1)}, bf16[3,2048,1024]{2,1,0:T(8,128)(2,1)}, u32[]{:S(2)}, u32[]{:S(2)}) collective-permute-start(bf16[3,2048,1024]{2,1,0:T(8,128)(2,1)} %collective-permute-done.1), channel_id=1, source_target_pairs={{0,8},{8,16},{16,24},{24,0},{1,9},{9,17},{17,25},{25,1},{2,10},{10... | collective-permute-start | bytes 37748744 | tf_op jit(solution)/shard_map/ppermute | solution.py:17
  587.9 6.9 copy-start
  607.7 237.9 %copy-start.2 = (f32[16,1024]{1,0:T(8,128)S(1)}, f32[16,1024]{1,0:T(8,128)}, u32[]{:S(2)}) copy-start(f32[16,1024]{1,0:T(8,128)} %param.11) | copy-start | bytes 196612
  830.0 16.3 %collective-permute-start.3 = (bf16[3,2,1024]{2,1,0:T(2,128)(2,1)S(1)}, bf16[3,2,1024]{2,1,0:T(2,128)(2,1)S(1)}, u32[]{:S(2)}, u32[]{:S(2)}) collective-permute-start(bf16[3,2,1024]{2,1,0:T(2,128)(2,1)S(1)} %slice.40), channel_id=1, source_target_pairs={{0,8},{8,16},{16,24},{1,9},{9,17},{17,25},{2,10},{10,18},{18,26},{... | collective-permute-start | bytes 36872 | tf_op jit(solution)/shard_map/ppermute | solution.py:28
  847.6 3.7 copy-start.3
  871.1 3.9 copy-start.4
  889.0 2.8 copy-start.1
  889.0 2.8 copy-start.5
Sparse Core Ops, SparseCore 0:
  283.3 304.5 all-gather.3
